TPU v7x, 32 devices: a whole 2x2x4 slice. The times are simulated.
32 devices in a mesh: groups: 2 (over y), space: 8 (over z, x), tm: 2 (over core).
Axes of the slice: x: 2, y: 2, z: 4, core: 2. Of those that a mesh axis runs over, the one named last changes fastest.
Arguments:
- latents: bfloat16 [4, 16, 4, 256, 256], P('groups', 'space', 'tm'), parts along dimension 0, may hold values from -6 to 6
- cotangent: bfloat16 [4, 16, 4, 256, 256], P('groups', 'space', 'tm'), parts along dimension 0, may hold values from -6 to 6
- valid_frames: int32 [4], P('groups'), parts along dimension 0, may hold values from 1 to 16, as said below
- spatial_weight: bfloat16 [9, 256, 256], replicated, may hold values from -0.125 to 0.125
- temporal_weight: bfloat16 [3, 256, 256], replicated, may hold values from -0.21875 to 0.21875
- cond_weight: bfloat16 [256, 256], replicated, may hold values from -0.375 to 0.375
Outputs:
- output: bfloat16 [4, 16, 4, 256, 256], P('groups', 'space', 'tm'), parts along dimension 0
- grad_latents: bfloat16 [4, 16, 4, 256, 256], P('groups', 'space', 'tm'), parts along dimension 0
- grad_spatial: bfloat16 [18, 256, 256], P('groups'), parts along dimension 0
- grad_temporal: bfloat16 [6, 256, 256], P('groups'), parts along dimension 0
- grad_cond: bfloat16 [512, 256], P('groups'), parts along dimension 0
There are 2 independent parts, one for each index of `groups`. A program takes and returns all parts, laid end to end along the dimension named above; an argument that names none is the same for every part. Nothing has to cross between parts.
Inputs may be any that keep to these rules, and one draw needn't show every extreme that they name: `valid_frames`: the first clip has all 16 frames valid; the others have 1 to 16.
All inputs are finite; a program needn't handle non-finite values.
Results may differ from a plain program's by a relative error of at most 0.0055.
Values may be sent and summed in bfloat16 or wider, within the bound.
No kernel may reach another device: no remote copies, remote signals or barrier semaphores. Data moves between devices by JAX's collectives and lax.ppermute only.
A program may use at most 128 MiB of HBM per device.

v0:
```python
import jax
import jax.numpy as jnp
from jax import lax
from jax.sharding import PartitionSpec as P


def from_root(block, axis, source):
    block = jnp.where(lax.axis_index(axis) == source, block, jnp.zeros_like(block))
    return lax.psum(block, axis)


def shifted(value, axis, by):
    count = lax.axis_size(axis)
    pairs = [(i, i + by) for i in range(count) if 0 <= i + by < count]
    return lax.ppermute(value, axis, pairs)


def spatial_sum(padded, weights, flip):
    rows = padded.shape[2] - 2
    cols = padded.shape[3] - 2
    total = jnp.zeros(padded.shape[:2] + (rows, cols, weights.shape[2]), jnp.float32)
    for row_off in range(3):
        for col_off in range(3):
            if flip:
                piece = padded[
                    :, :, 2 - row_off : 2 - row_off + rows, 2 - col_off : 2 - col_off + cols
                ]
                kernel = weights[3 * row_off + col_off].T
            else:
                piece = padded[:, :, row_off : row_off + rows, col_off : col_off + cols]
                kernel = weights[3 * row_off + col_off]
            total = total + jnp.dot(piece, kernel, preferred_element_type=jnp.float32)
    return total


def lag_forward(padded_act, weights, count):
    total = 0.0
    for lag in range(3):
        total = total + jnp.dot(
            padded_act[:, 2 - lag : 2 - lag + count],
            weights[lag],
            preferred_element_type=jnp.float32,
        )
    return total


def lag_backward(padded_cot, weights, count):
    total = 0.0
    for lag in range(3):
        total = total + jnp.dot(
            padded_cot[:, lag : lag + count], weights[lag].T, preferred_element_type=jnp.float32
        )
    return total


def lag_grads(padded_act, cot, count):
    dims = (((0, 1, 2, 3), (0, 1, 2, 3)), ((), ()))
    terms = []
    for lag in range(3):
        terms.append(
            lax.dot_general(
                padded_act[:, 2 - lag : 2 - lag + count],
                cot,
                dims,
                preferred_element_type=jnp.float32,
            )
        )
    return jnp.stack(terms)


def own_window(whole, rows):
    padded_rows = jnp.pad(whole, ((0, 0), (0, 0), (1, 1), (0, 0), (0, 0)))
    start = lax.axis_index("tm") * rows
    return lax.dynamic_slice_in_dim(padded_rows, start, rows + 2, 2)


def on_device(latents, cotangent, valid_frames, spatial_weight, temporal_weight, cond_weight):
    clips, frames, rows, cols, chans = latents.shape
    slab = lax.axis_index("space")
    frame_ids = slab * frames + jnp.arange(frames, dtype=jnp.int32)
    mask = (frame_ids[None, :] < valid_frames[:, None]).astype(jnp.bfloat16)[:, :, None, None, None]
    mask_f = mask.astype(jnp.float32)
    masked = latents * mask
    first = from_root(masked[:, 0], "space", 0)
    rows_pad = own_window(lax.all_gather(masked, "tm", axis=2, tiled=True), rows)
    padded = jnp.pad(rows_pad, ((0, 0), (0, 0), (0, 0), (1, 1), (0, 0)))
    pre = spatial_sum(padded, spatial_weight, False)
    act = jax.nn.silu(pre).astype(jnp.bfloat16)
    cot = cotangent * mask
    earlier = shifted(act, "space", 1)
    act_pad = jnp.concatenate([earlier, act], axis=1)
    mixed = lag_forward(act_pad, temporal_weight, frames)
    later = shifted(cot, "space", -1)
    cot_pad = jnp.concatenate([cot, later], axis=1)
    dact = lag_backward(cot_pad, temporal_weight, frames)
    temporal_terms = lag_grads(act_pad, cot, frames)
    cond = jnp.dot(first, cond_weight, preferred_element_type=jnp.float32)
    output = ((masked.astype(jnp.float32) + mixed + cond[:, None]) * mask_f).astype(jnp.bfloat16)
    sig = jax.nn.sigmoid(pre)
    dpre = (dact * sig * (1.0 + pre * (1.0 - sig))).astype(jnp.bfloat16)
    cot_sum = lax.psum(jnp.sum(cot, axis=1, dtype=jnp.float32), "space")
    cond_back = jnp.dot(cot_sum, cond_weight.astype(jnp.float32).T, precision=lax.Precision.HIGHEST)
    dpre_rows = own_window(lax.all_gather(dpre, "tm", axis=2, tiled=True), rows)
    dpre_pad = jnp.pad(dpre_rows, ((0, 0), (0, 0), (0, 0), (1, 1), (0, 0)))
    dmasked = spatial_sum(dpre_pad, spatial_weight, True)
    is_first = (frame_ids == 0).astype(jnp.float32)[None, :, None, None, None]
    grad_latents = (
        (cot.astype(jnp.float32) + dmasked + is_first * cond_back[:, None]) * mask_f
    ).astype(jnp.bfloat16)
    dims = (((0, 1, 2, 3), (0, 1, 2, 3)), ((), ()))
    spatial_terms = []
    for row_off in range(3):
        for col_off in range(3):
            piece = padded[:, :, row_off : row_off + rows, col_off : col_off + cols]
            spatial_terms.append(
                lax.dot_general(piece, dpre, dims, preferred_element_type=jnp.float32)
            )
    spatial_terms = jnp.stack(spatial_terms)
    is_owner = (slab == 0).astype(jnp.float32)
    cond_terms = is_owner * lax.dot_general(
        first.astype(jnp.float32),
        cot_sum,
        (((0, 1, 2), (0, 1, 2)), ((), ())),
        precision=lax.Precision.HIGHEST,
    )
    summed = lax.psum((spatial_terms, temporal_terms, cond_terms), ("space", "tm"))
    scale = (clips * frames * rows * cols * lax.axis_size("space") * lax.axis_size("tm")) ** (-0.5)
    grad_spatial = (summed[0] * scale).astype(jnp.bfloat16)
    grad_temporal = (summed[1] * scale).astype(jnp.bfloat16)
    grad_cond = (summed[2] * scale).astype(jnp.bfloat16)
    return (output, grad_latents, grad_spatial, grad_temporal, grad_cond)


def solution(mesh):
    return jax.shard_map(
        on_device,
        mesh=mesh,
        in_specs=(
            P("groups", "space", "tm", None, None),
            P("groups", "space", "tm", None, None),
            P("groups"),
            P(),
            P(),
            P(),
        ),
        out_specs=(
            P("groups", "space", "tm", None, None),
            P("groups", "space", "tm", None, None),
            P("groups", None, None),
            P("groups", None, None),
            P("groups", None),
        ),
        check_vma=False,
    )
```

profile of v0, /device:TPU:0, one launch (start us, length us, event | category | flops | bytes accessed | tf_op | source)
XLA Modules:
  0.0 338.7 jit_solution(10557166967447815481)
XLA Ops:
  8.8 1.4 broadcast_multiply_fusion.1
  11.2 2.7 convert_reduce_fusion
  14.5 1.3 collective-permute-start.1
  15.9 1.8 fusion.75
  17.7 75.7 %all-reduce.9.cloned.1.call-done = bf16[2,2,256,256]{3,2,1,0:T(8,128)(2,1)} async-done(((bf16[2,2,256,256]{3,2,1,0:T(8,128)(2,1)}), bf16[2,2,256,256]{3,2,1,0:T(8,128)(2,1)}) %all-reduce.9.cloned.1.call-update) | async-done | bytes 524304 | tf_op jit(solution)/shard_map/psum | solution.py:9
  93.3 2.3 fusion.47
  95.7 79.6 %all-reduce.11.cloned.1.call-done = f32[2,2,256,256]{3,2,1,0:T(8,128)} async-done(((f32[2,2,256,256]{3,2,1,0:T(8,128)}), f32[2,2,256,256]{3,2,1,0:T(8,128)}) %all-reduce.11.cloned.1.call-update) | async-done | bytes 1048592 | tf_op jit(solution)/shard_map/psum | solution.py:101
  175.3 3.0 fusion.13
  178.2 1.6 fusion.45
  179.9 1.8 fusion.3
  181.7 1.8 pad_dynamic-slice_fusion.1
  187.1 2.1 multiply_convert_fusion.3
  189.9 2.0 multiply_convert_fusion.1
  191.9 1.2 fusion.19
  193.2 3.5 %collective-permute-start = (bf16[2,2,2,256,256]{4,3,2,1,0:T(8,128)(2,1)}, bf16[2,2,2,256,256]{4,3,2,1,0:T(8,128)(2,1)S(1)}, u32[]{:S(2)}, u32[]{:S(2)}) collective-permute-start(bf16[2,2,2,256,256]{4,3,2,1,0:T(8,128)(2,1)} %get-tuple-element.12), channel_id=1, source_target_pairs={{0,2},{2,4},{4,6},{6,8},{8,10},{10,12},{12,14},{1,3},{3,5},{5,7},{... | collective-permute-start | bytes 3145736 | tf_op jit(solution)/shard_map/ppermute | solution.py:15
  196.7 2.4 fusion.12
  199.1 1.2 fusion.18
  200.3 1.2 fusion.17
  201.5 1.2 fusion.11
  202.7 1.2 fusion.16
  203.8 1.2 fusion.15
  205.9 1.2 fusion.10
  207.1 1.2 fusion.14
  208.3 2.7 fusion.77
  211.0 7.8 %collective-permute-done = bf16[2,2,2,256,256]{4,3,2,1,0:T(8,128)(2,1)S(1)} collective-permute-done((bf16[2,2,2,256,256]{4,3,2,1,0:T(8,128)(2,1)}, bf16[2,2,2,256,256]{4,3,2,1,0:T(8,128)(2,1)S(1)}, u32[]{:S(2)}, u32[]{:S(2)}) %collective-permute-start) | collective-permute-done | bytes 1048608 | tf_op jit(solution)/shard_map/ppermute | solution.py:15
  219.8 1.0 pad_maximum_fusion.5
  220.8 1.2 copy-done.8
  224.6 1.7 multiply_convert_fusion.2
  226.3 1.8 pad_dynamic-slice_fusion
  233.1 2.2 fusion.2
  235.3 91.7 %all-reduce.13.cloned.1.call-done = (f32[9,256,256]{2,1,0:T(8,128)}, f32[3,256,256]{2,1,0:T(8,128)}, f32[256,256]{1,0:T(8,128)}) async-done(((f32[9,256,256]{2,1,0:T(8,128)}, f32[3,256,256]{2,1,0:T(8,128)}, f32[256,256]{1,0:T(8,128)}), (f32[9,256,256]{2,1,0:T(8,128)}, f32[3,256,256]{2,1,0:T(8,128)}, f32[256,256]{1,0:T(8,128)})) %all-reduce.13.cloned.1.call-update) | async-done | bytes 3407888 | tf_op jit(solution)/shard_map/psum | solution.py:126
  327.0 3.0 multiply_convert_fusion
  (92 shorter events, 17.6 us)
Async XLA Ops:
  8.0 85.3 %copy-start = (bf16[256,256]{1,0:T(8,128)(2,1)S(1)}, bf16[256,256]{1,0:T(8,128)(2,1)}, u32[]{:S(2)}) copy-start(bf16[256,256]{1,0:T(8,128)(2,1)} %param.11) | copy-start | bytes 393220
  8.0 85.3 %all-reduce.9.cloned.1.call-start = ((), (), s32[]{:S(2)}) async-start(), calls=%async_computation.1 | async-start | bytes 1048576 | tf_op jit(solution)/shard_map/psum | solution.py:9
  10.2 3.7 %copy-start.11 = (bf16[2,2,2,256,256]{4,3,2,1,0:T(8,128)(2,1)}, bf16[2,2,2,256,256]{4,3,2,1,0:T(8,128)(2,1)S(1)}, u32[]{:S(2)}) copy-start(bf16[2,2,2,256,256]{4,3,2,1,0:T(8,128)(2,1)S(1)} %broadcast_multiply_fusion.1) | copy-start | bytes 3145732
  11.1 4.8 %copy-start.21 = (bf16[3,256,256]{2,1,0:T(8,128)(2,1)S(1)}, bf16[3,256,256]{2,1,0:T(8,128)(2,1)}, u32[]{:S(2)}) copy-start(bf16[3,256,256]{2,1,0:T(8,128)(2,1)} %param.10) | copy-start | bytes 1179652
  11.1 164.2 %all-reduce.11.cloned.1.call-start = ((), (), s32[]{:S(2)}) async-start(), calls=%async_computation.3 | async-start | bytes 2097152 | tf_op jit(solution)/shard_map/psum | solution.py:101
  13.9 166.0 %copy-start.4 = (bf16[2,2,2,256,256]{4,3,2,1,0:T(8,128)(2,1)}, bf16[2,2,2,256,256]{4,3,2,1,0:T(8,128)(2,1)S(1)}, u32[]{:S(2)}) copy-start(bf16[2,2,2,256,256]{4,3,2,1,0:T(8,128)(2,1)S(1)} %get-tuple-element.9) | copy-start | bytes 3145732
  13.9 167.8 %all-gather.3.cloned.1.call-start = ((), (), s32[]{:S(2)}) async-start(), calls=%async_computation | async-start | bytes 3145728 | tf_op jit(solution)/shard_map/all_gather | solution.py:85
  14.5 211.8 %all-gather.5.cloned.1.call-start = ((), (), s32[]{:S(2)}) async-start(), calls=%async_computation.2 | async-start | bytes 3145728 | tf_op jit(solution)/shard_map/all_gather | solution.py:103
  14.5 165.3 %collective-permute-start.1 = (bf16[2,2,2,256,256]{4,3,2,1,0:T(8,128)(2,1)S(1)}, bf16[2,2,2,256,256]{4,3,2,1,0:T(8,128)(2,1)S(1)}, u32[]{:S(2)}, u32[]{:S(2)}) collective-permute-start(bf16[2,2,2,256,256]{4,3,2,1,0:T(8,128)(2,1)S(1)} %get-tuple-element.9), channel_id=1, source_target_pairs={{2,0},{4,2},{6,4},{8,6},{10,8},{12,10},{14,12},{3,1},{5,3},{7,5},{... | collective-permute-start | bytes 3145736 | tf_op jit(solution)/shard_map/ppermute | solution.py:15
  175.3 3.0 copy-start.18
  179.8 1.8 copy-start.23
  181.7 1.8 copy-start.14
  187.1 2.2 copy-start.19
  187.1 2.3 copy-start.20
  187.1 2.8 copy-start.24
  193.1 6.0 %copy-start.3 = (bf16[2,2,2,256,256]{4,3,2,1,0:T(8,128)(2,1)S(1)}, bf16[2,2,2,256,256]{4,3,2,1,0:T(8,128)(2,1)}, u32[]{:S(2)}) copy-start(bf16[2,2,2,256,256]{4,3,2,1,0:T(8,128)(2,1)} %copy-done.2) | copy-start | bytes 3145732
  193.2 133.8 %all-reduce.13.cloned.1.call-start = ((), (), s32[]{:S(2)}) async-start(), calls=%async_computation.4 | async-start | bytes 6815744 | tf_op jit(solution)/shard_map/psum | solution.py:126
  193.2 25.7 %collective-permute-start = (bf16[2,2,2,256,256]{4,3,2,1,0:T(8,128)(2,1)}, bf16[2,2,2,256,256]{4,3,2,1,0:T(8,128)(2,1)S(1)}, u32[]{:S(2)}, u32[]{:S(2)}) collective-permute-start(bf16[2,2,2,256,256]{4,3,2,1,0:T(8,128)(2,1)} %get-tuple-element.12), channel_id=1, source_target_pairs={{0,2},{2,4},{4,6},{6,8},{8,10},{10,12},{12,14},{1,3},{3,5},{5,7},{... | collective-permute-start | bytes 3145736 | tf_op jit(solution)/shard_map/ppermute | solution.py:15
  203.8 1.2 copy-start.5
  203.8 1.6 copy-start.7
  220.8 1.2 copy-start.8
  220.8 1.5 copy-start.10
  220.8 1.6 copy-start.22
  222.4 1.2 copy-start.12
  222.4 1.9 copy-start.13
  222.4 2.2 copy-start.17
  226.3 1.9 copy-start.15
  231.6 1.2 copy-start.6
  231.6 1.6 copy-start.16
  327.0 3.0 copy-start.25
  327.0 4.5 %copy-start.1 = (bf16[256,256]{1,0:T(8,128)(2,1)S(1)}, bf16[256,256]{1,0:T(8,128)(2,1)}, u32[]{:S(2)}) copy-start(bf16[256,256]{1,0:T(8,128)(2,1)} %param.11) | copy-start | bytes 393220
  327.0 3.9 %copy-start.26 = (f32[256,256]{1,0:T(8,128)S(1)}, f32[256,256]{1,0:T(8,128)}, u32[]{:S(2)}) copy-start(f32[256,256]{1,0:T(8,128)} %get-tuple-element.7) | copy-start | bytes 786436
  (2 other events, 2.2 us)
Sparse Core Ops, SparseCore 0:
  12.8 80.4 all-reduce.8
  97.8 77.4 all-reduce.10
  220.9 105.9 all-reduce.12
Sparse Core Ops, SparseCore 1:
  16.5 13.1 all-gather.2
  193.2 10.0 all-gather.4
where the time goes:
time: 339 us
  waiting for transfers between devices  255 us (75%)
  matrix products  42.3 us (12%)
  between operations  15.5 us (5%)
  other arithmetic  11.2 us (3%)
  local copies, waits for them, and re-layouts  9.27 us (3%)
  starting transfers between devices  5.03 us (1%)
    psum x1, waiting for transfers between devices, on_device(): lax.psum((spatial_terms, temporal_terms, cond_terms), ('space', 'tm'))  91.7 us
    psum x1, waiting for transfers between devices, on_device(): cot_sum = lax.psum(jnp.sum(cot, axis=1, dtype=jnp.float32), 'space')  79.6 us
    psum x1, waiting for transfers between devices, from_root(): return lax.psum(block, axis)  75.7 us
    dot_general x9, matrix products, on_device(): lax.dot_general(piece, dpre, dims, preferred_element_type=jnp.float32)  11.9 us
    dot_general x18, matrix products, spatial_sum(): total = total + jnp.dot(piece, kernel, preferred_element_type=jnp.float32)  11.7 us
    ppermute x2, waiting for transfers between devices, shifted(): return lax.ppermute(value, axis, pairs)  7.84 us
  transfers between devices with their start and end apart: 7, of which 4 were waited for; matrix products, arithmetic and copies ran while one was open for 12% of the time, Pallas kernels for 0%

commit v1 on v0

--- a/solution.py
+++ b/solution.py
@@ -123,7 +123,7 @@
         (((0, 1, 2), (0, 1, 2)), ((), ())),
         precision=lax.Precision.HIGHEST,
     )
-    summed = lax.psum((spatial_terms, temporal_terms, cond_terms), ("space", "tm"))
+    summed = lax.psum(lax.psum((spatial_terms, temporal_terms, cond_terms), "tm"), "space")
     scale = (clips * frames * rows * cols * lax.axis_size("space") * lax.axis_size("tm")) ** (-0.5)
     grad_spatial = (summed[0] * scale).astype(jnp.bfloat16)
     grad_temporal = (summed[1] * scale).astype(jnp.bfloat16)

time: 339 us -> 393 us (1.16)
  waiting for transfers between devices: 255 us -> 316 us
  matrix products: 42.3 us -> 37.4 us
    psum x1 -> x2, waiting for transfers between devices: 91.7 us -> 132 us  [the longest x1 117 us: on_device(): lax.psum(lax.psum((spatial_terms, temporal_terms, cond_terms), 'tm'), 'sp...]
    all_gather x1, waiting for transfers between devices: 0.01 us -> 13.2 us  [on_device(): dpre_rows = own_window(lax.all_gather(dpre, 'tm', axis=2, tiled=True), rows)]
    dot_general x9, matrix products: 11.9 us -> 4.35 us  [on_device(): lax.dot_general(piece, dpre, dims, preferred_element_type=jnp.float32)]
    ppermute x2, waiting for transfers between devices: 7.84 us -> 12.5 us  [shifted(): return lax.ppermute(value, axis, pairs)]
  transfers between devices with their start and end apart: 7 -> 8, of which waited for: 4 -> 6; matrix products, arithmetic and copies ran while one was open for 12% -> 8% of each run, Pallas kernels for 0% -> 0%
where the time goes in v1:
time: 393 us
  waiting for transfers between devices  316 us (80%)
  matrix products  37.4 us (10%)
  between operations  15.8 us (4%)
  other arithmetic  11.2 us (3%)
  local copies, waits for them, and re-layouts  6.24 us (2%)
  starting transfers between devices  5.9 us (2%)
    psum x1, waiting for transfers between devices, on_device(): lax.psum(lax.psum((spatial_terms, temporal_terms, cond_terms), 'tm'), 'sp...  117 us
    psum x1, waiting for transfers between devices, on_device(): cot_sum = lax.psum(jnp.sum(cot, axis=1, dtype=jnp.float32), 'space')  81.9 us
    psum x1, waiting for transfers between devices, from_root(): return lax.psum(block, axis)  75.1 us
    psum x1, waiting for transfers between devices, on_device(): lax.psum((spatial_terms, temporal_terms, cond_terms), 'tm')  15.4 us
    all_gather x1, waiting for transfers between devices, on_device(): dpre_rows = own_window(lax.all_gather(dpre, 'tm', axis=2, tiled=True), rows)  13.2 us
    ppermute x2, waiting for transfers between devices, shifted(): return lax.ppermute(value, axis, pairs)  12.5 us
    dot_general x18, matrix products, spatial_sum(): total = total + jnp.dot(piece, kernel, preferred_element_type=jnp.float32)  11.9 us
  transfers between devices with their start and end apart: 8, of which 6 were waited for; matrix products, arithmetic and copies ran while one was open for 8% of the time, Pallas kernels for 0%

profile of v1, /device:TPU:0, one launch (start us, length us, event | category | flops | bytes accessed | tf_op | source)
XLA Modules:
  0.0 392.5 jit_solution(5136906398002696829)
XLA Ops:
  8.1 0.7 fusion.124
  8.8 1.4 broadcast_multiply_fusion.1
  10.2 0.9 fusion.44
  11.2 2.7 convert_reduce_fusion
  14.6 1.3 collective-permute-start.1
  15.9 1.8 fusion.75
  17.7 75.1 %all-reduce.11.cloned.1.call-done = bf16[2,2,256,256]{3,2,1,0:T(8,128)(2,1)} async-done(((bf16[2,2,256,256]{3,2,1,0:T(8,128)(2,1)}), bf16[2,2,256,256]{3,2,1,0:T(8,128)(2,1)}) %all-reduce.11.cloned.1.call-update) | async-done | bytes 524304 | tf_op jit(solution)/shard_map/psum | solution.py:9
  92.9 81.9 %all-reduce.13.cloned.1.call-done = f32[2,2,256,256]{3,2,1,0:T(8,128)} async-done(((f32[2,2,256,256]{3,2,1,0:T(8,128)}), f32[2,2,256,256]{3,2,1,0:T(8,128)}) %all-reduce.13.cloned.1.call-update) | async-done | bytes 1048592 | tf_op jit(solution)/shard_map/psum | solution.py:101
  174.8 2.9 fusion.13
  177.7 1.1 copy-done.16
  178.8 1.8 fusion.3
  180.6 1.8 pad_dynamic-slice_fusion.1
  186.0 2.2 multiply_convert_fusion.3
  188.1 4.1 %collective-permute-start = (bf16[2,2,2,256,256]{4,3,2,1,0:T(8,128)(2,1)}, bf16[2,2,2,256,256]{4,3,2,1,0:T(8,128)(2,1)}, u32[]{:S(2)}, u32[]{:S(2)}) collective-permute-start(bf16[2,2,2,256,256]{4,3,2,1,0:T(8,128)(2,1)} %get-tuple-element.15), channel_id=1, source_target_pairs={{0,2},{2,4},{4,6},{6,8},{8,10},{10,12},{12,14},{1,3},{3,5},{5,7},{... | collective-permute-start | bytes 3145736 | tf_op jit(solution)/shard_map/ppermute | solution.py:15
  192.3 2.0 multiply_convert_fusion.1
  197.2 0.7 copy-done.3
  198.0 1.7 convolution_bitcast_fusion.5
  201.2 12.5 %collective-permute-done = bf16[2,2,2,256,256]{4,3,2,1,0:T(8,128)(2,1)} collective-permute-done((bf16[2,2,2,256,256]{4,3,2,1,0:T(8,128)(2,1)}, bf16[2,2,2,256,256]{4,3,2,1,0:T(8,128)(2,1)}, u32[]{:S(2)}, u32[]{:S(2)}) %collective-permute-start) | collective-permute-done | bytes 1048608 | tf_op jit(solution)/shard_map/ppermute | solution.py:15
  213.7 1.7 fusion.9
  215.4 1.7 convolution_bitcast_fusion.4
  217.1 0.9 pad_maximum_fusion.5
  220.0 1.7 fusion.77
  221.7 1.7 fusion.7
  223.4 3.2 multiply_convert_fusion.2
  226.7 15.4 %all-reduce.17.cloned.1.call-done = (f32[9,256,256]{2,1,0:T(8,128)}, f32[3,256,256]{2,1,0:T(8,128)}, f32[256,256]{1,0:T(8,128)}) async-done(((f32[9,256,256]{2,1,0:T(8,128)}, f32[3,256,256]{2,1,0:T(8,128)}, f32[256,256]{1,0:T(8,128)}), (f32[9,256,256]{2,1,0:T(8,128)}, f32[3,256,256]{2,1,0:T(8,128)}, f32[256,256]{1,0:T(8,128)})) %all-reduce.17.cloned.1.call-update) | async-done | bytes 3407888 | tf_op jit(solution)/shard_map/psum | solution.py:126
  242.1 13.2 %all-gather.5.cloned.1.call-done = bf16[2,2,4,256,256]{4,3,2,1,0:T(8,128)(2,1)} async-done(((bf16[2,2,2,256,256]{4,3,2,1,0:T(8,128)(2,1)}), bf16[2,2,4,256,256]{4,3,2,1,0:T(8,128)(2,1)}) %all-gather.5.cloned.1.call-update) | async-done | bytes 2097168 | tf_op jit(solution)/shard_map/all_gather | solution.py:103
  255.3 1.7 pad_dynamic-slice_fusion
  260.8 0.8 copy-done.4
  261.6 2.4 fusion.2
  263.9 116.7 %all-reduce.15.cloned.1.call-done = (f32[9,256,256]{2,1,0:T(8,128)}, f32[3,256,256]{2,1,0:T(8,128)}, f32[256,256]{1,0:T(8,128)}) async-done(((f32[9,256,256]{2,1,0:T(8,128)}, f32[3,256,256]{2,1,0:T(8,128)}, f32[256,256]{1,0:T(8,128)}), (f32[9,256,256]{2,1,0:T(8,128)}, f32[3,256,256]{2,1,0:T(8,128)}, f32[256,256]{1,0:T(8,128)})) %all-reduce.15.cloned.1.call-update) | async-done | bytes 3407888 | tf_op jit(solution)/shard_map/psum | solution.py:126
  380.6 3.0 multiply_convert_fusion
  383.7 0.8 multiply_convert_fusion.4
  (81 shorter events, 15.2 us)
Async XLA Ops:
  8.0 210.9 %copy-start = (bf16[256,256]{1,0:T(8,128)(2,1)S(1)}, bf16[256,256]{1,0:T(8,128)(2,1)}, u32[]{:S(2)}) copy-start(bf16[256,256]{1,0:T(8,128)(2,1)} %param.11) | copy-start | bytes 393220
  8.0 84.9 %all-reduce.11.cloned.1.call-start = ((), (), s32[]{:S(2)}) async-start(), calls=%async_computation.1 | async-start | bytes 1048576 | tf_op jit(solution)/shard_map/psum | solution.py:9
  10.2 3.7 copy-start.5
  11.1 4.8 %copy-start.14 = (bf16[3,256,256]{2,1,0:T(8,128)(2,1)S(1)}, bf16[3,256,256]{2,1,0:T(8,128)(2,1)}, u32[]{:S(2)}) copy-start(bf16[3,256,256]{2,1,0:T(8,128)(2,1)} %param.10) | copy-start | bytes 1179652
  11.1 163.7 %all-reduce.13.cloned.1.call-start = ((), (), s32[]{:S(2)}) async-start(), calls=%async_computation.3 | async-start | bytes 2097152 | tf_op jit(solution)/shard_map/psum | solution.py:101
  13.9 163.8 %copy-start.2 = (bf16[2,2,2,256,256]{4,3,2,1,0:T(8,128)(2,1)}, bf16[2,2,2,256,256]{4,3,2,1,0:T(8,128)(2,1)S(1)}, u32[]{:S(2)}) copy-start(bf16[2,2,2,256,256]{4,3,2,1,0:T(8,128)(2,1)S(1)} %get-tuple-element.12) | copy-start | bytes 3145732
  13.9 166.7 %all-gather.3.cloned.1.call-start = ((), (), s32[]{:S(2)}) async-start(), calls=%async_computation | async-start | bytes 3145728 | tf_op jit(solution)/shard_map/all_gather | solution.py:85
  14.5 227.5 %all-reduce.17.cloned.1.call-start = ((), (), s32[]{:S(2)}) async-start(), calls=%async_computation.5 | async-start | bytes 6815744 | tf_op jit(solution)/shard_map/psum | solution.py:126
  14.6 163.1 %collective-permute-start.1 = (bf16[2,2,2,256,256]{4,3,2,1,0:T(8,128)(2,1)S(1)}, bf16[2,2,2,256,256]{4,3,2,1,0:T(8,128)(2,1)S(1)}, u32[]{:S(2)}, u32[]{:S(2)}) collective-permute-start(bf16[2,2,2,256,256]{4,3,2,1,0:T(8,128)(2,1)S(1)} %get-tuple-element.12), channel_id=1, source_target_pairs={{2,0},{4,2},{6,4},{8,6},{10,8},{12,10},{14,12},{3,1},{5,3},{7,5},{... | collective-permute-start | bytes 3145736 | tf_op jit(solution)/shard_map/ppermute | solution.py:15
  177.7 1.1 copy-start.16
  180.6 1.8 copy-start.7
  186.0 6.3 %copy-start.11 = (f32[2,2,2,256,256]{4,3,2,1,0:T(8,128)S(1)}, f32[2,2,2,256,256]{4,3,2,1,0:T(8,128)}, u32[]{:S(2)}) copy-start(f32[2,2,2,256,256]{4,3,2,1,0:T(8,128)} %fusion.75) | copy-start | bytes 6291460
  186.0 6.3 %copy-start.12 = (f32[2,2,2,256,256]{4,3,2,1,0:T(8,128)S(1)}, f32[2,2,2,256,256]{4,3,2,1,0:T(8,128)}, u32[]{:S(2)}) copy-start(f32[2,2,2,256,256]{4,3,2,1,0:T(8,128)} %fusion.3) | copy-start | bytes 6291460
  186.0 6.3 %copy-start.17 = (bf16[2,2,2,256,256]{4,3,2,1,0:T(8,128)(2,1)S(1)}, bf16[2,2,2,256,256]{4,3,2,1,0:T(8,128)(2,1)}, u32[]{:S(2)}) copy-start(bf16[2,2,2,256,256]{4,3,2,1,0:T(8,128)(2,1)} %copy-done.16) | copy-start | bytes 3145732
  188.1 25.5 %collective-permute-start = (bf16[2,2,2,256,256]{4,3,2,1,0:T(8,128)(2,1)}, bf16[2,2,2,256,256]{4,3,2,1,0:T(8,128)(2,1)}, u32[]{:S(2)}, u32[]{:S(2)}) collective-permute-start(bf16[2,2,2,256,256]{4,3,2,1,0:T(8,128)(2,1)} %get-tuple-element.15), channel_id=1, source_target_pairs={{0,2},{2,4},{4,6},{6,8},{8,10},{10,12},{12,14},{1,3},{3,5},{5,7},{... | collective-permute-start | bytes 3145736 | tf_op jit(solution)/shard_map/ppermute | solution.py:15
  194.3 6.4 %copy-start.1 = (bf16[2,2,2,256,256]{4,3,2,1,0:T(8,128)(2,1)}, bf16[2,2,2,256,256]{4,3,2,1,0:T(8,128)(2,1)S(1)}, u32[]{:S(2)}) copy-start(bf16[2,2,2,256,256]{4,3,2,1,0:T(8,128)(2,1)S(1)} %multiply_convert_fusion.1) | copy-start | bytes 3145732
  196.7 1.2 copy-start.3
  201.1 15.9 %copy-start.10 = (f32[9,256,256]{2,1,0:T(8,128)}, f32[9,256,256]{2,1,0:T(8,128)S(1)}, u32[]{:S(2)}) copy-start(f32[9,256,256]{2,1,0:T(8,128)S(1)} %fusion.14) | copy-start | bytes 7077892
  218.0 1.0 copy-start.13
  218.0 1.4 copy-start.9
  218.0 37.2 %all-gather.5.cloned.1.call-start = ((), (), s32[]{:S(2)}) async-start(), calls=%async_computation.2 | async-start | bytes 3145728 | tf_op jit(solution)/shard_map/all_gather | solution.py:103
  218.6 1.4 copy-start.15
  218.6 162.0 %all-reduce.15.cloned.1.call-start = ((), (), s32[]{:S(2)}) async-start(), calls=%async_computation.4 | async-start | bytes 6815744 | tf_op jit(solution)/shard_map/psum | solution.py:126
  221.7 1.7 copy-start.6
  242.1 14.9 %copy-start.8 = (bf16[9,256,256]{2,1,0:T(8,128)(2,1)S(1)}, bf16[9,256,256]{2,1,0:T(8,128)(2,1)}, u32[]{:S(2)}) copy-start(bf16[9,256,256]{2,1,0:T(8,128)(2,1)} %param.9) | copy-start | bytes 3538948
  260.3 1.2 copy-start.4
  380.6 3.0 copy-start.18
  380.6 3.9 copy-start.19
Sparse Core Ops, SparseCore 0:
  12.3 80.5 all-reduce.10
  97.4 77.4 all-reduce.12
  242.2 138.3 all-reduce.14
Sparse Core Ops, SparseCore 1:
  16.5 13.1 all-gather.2
  218.1 23.9 all-reduce.16
  243.5 11.7 all-gather.4
